TPU v7x, 32 devices: a whole 2x2x4 slice. The times are simulated.
32 devices in a mesh: dp: 4 (over z), fsdp: 2 (over x), rows: 4 (over y, core).
Axes of the slice: x: 2, y: 2, z: 4, core: 2. Of those that a mesh axis runs over, the one named last changes fastest.
Arguments:
- feature_maps: bfloat16 [8, 16, 32, 1536], P(('dp', 'fsdp'), 'rows'), may hold values from -30 to 30
- dw_kernel: float32 [7, 7, 1536], replicated, may hold values from -0.875 to 0.875
- norm_gain: float32 [1536], replicated, may hold values from 0.5 to 1.5
- w_up: bfloat16 [1536, 6144], P(('dp', 'rows'), 'fsdp'), may hold values from -0.15625 to 0.15625
- w_down: bfloat16 [6144, 1536], P('fsdp', ('dp', 'rows')), may hold values from -0.078125 to 0.078125
- layer_scale: float32 [1536], replicated, may hold values from 0.3 to 1.5
- d_out: bfloat16 [8, 16, 32, 1536], P(('dp', 'fsdp'), 'rows'), may hold values from -20 to 20
Outputs:
- result: bfloat16 [8, 16, 32, 1536], P(('dp', 'fsdp'), 'rows')
- grad_x: bfloat16 [8, 16, 32, 1536], P(('dp', 'fsdp'), 'rows')
- grad_up: float32 [1536, 6144], P(('dp', 'rows'), 'fsdp')
- grad_down: float32 [6144, 1536], P('fsdp', ('dp', 'rows'))
- grad_kernel: float32 [7, 7, 1536], replicated
- grad_gain: float32 [1536], replicated
- grad_scale: float32 [1536], replicated
All inputs are finite; a program needn't handle non-finite values.
Results may differ from a plain program's by a relative error of at most 0.0075.
Values may be sent and summed in bfloat16 or wider, within the bound.
No kernel may reach another device: no remote copies, remote signals or barrier semaphores. Data moves between devices by JAX's collectives and lax.ppermute only.
A program may use at most 128 MiB of HBM per device.

v0:
```python
import math
import jax
import jax.numpy as jnp
from jax import lax
from jax.sharding import PartitionSpec as P

KS = 7
norm_eps = 1e-06
inv_root_two = 1.0 / math.sqrt(2.0)
inv_root_two_pi = 1.0 / math.sqrt(2.0 * math.pi)
contract_rows = (((0,), (0,)), ((), ()))
contract_cols = (((1,), (1,)), ((), ()))


def padded_2(x, sides, width):
    for axis, dim in sides:
        devices, length = (lax.axis_size(axis), x.shape[dim])
        up = [(i, (i + 1) % devices) for i in range(devices - 1)]
        down = [(j, i) for i, j in up]
        last = lax.slice_in_dim(x, length - width, length, axis=dim)
        leading = lax.slice_in_dim(x, 0, width, axis=dim)
        before = lax.ppermute(last, axis, up)
        after = lax.ppermute(leading, axis, down)
        x = jnp.concatenate([before, x, after], axis=dim)
    return x


def gelu_exact(values):
    return 0.5 * values * (1.0 + jax.scipy.special.erf(values * inv_root_two))


def gelu_slope(values):
    cdf_part = 0.5 * (1.0 + jax.scipy.special.erf(values * inv_root_two))
    return cdf_part + values * jnp.exp(-0.5 * values * values) * inv_root_two_pi


def small_sums(kernel_part, gain_part, scale_part, width):
    every = ("dp", "fsdp", "rows")
    devices = lax.axis_size(every)
    packed = jnp.concatenate(
        [kernel_part.reshape(KS * KS, width), gain_part[None], scale_part[None]], axis=0
    )
    count = packed.shape[0]
    per = -(-count // devices)
    packed = jnp.pad(packed, ((0, per * devices - count), (0, 0)))
    mine = lax.all_to_all(packed.reshape(devices, per, width), every, 0, 0, tiled=True).sum(0)
    spread = jnp.broadcast_to(mine[None], (devices, per, width))
    total = lax.all_to_all(spread, every, 0, 0, tiled=True).reshape(devices * per, width)
    kernel_sum = total[: KS * KS].reshape(KS, KS, width)
    return (kernel_sum, total[KS * KS], total[KS * KS + 1])


def body(feature_maps, dw_kernel, norm_gain, w_up, w_down, layer_scale, d_out):
    scenes, strip, across, width = feature_maps.shape
    cells = scenes * strip * across
    hid_axes = ("fsdp", "rows")
    dp_size, row_size = (lax.axis_size("dp"), lax.axis_size("rows"))
    block_c, hid_f = w_up.shape
    sub = hid_f // row_size
    pieces = w_up.reshape(block_c, row_size, sub).transpose(1, 0, 2)
    pieces = jnp.broadcast_to(pieces[None], (dp_size, row_size, block_c, sub))
    pieces = pieces.reshape(dp_size * row_size, block_c, sub)
    up_loc = lax.all_to_all(pieces, ("dp", "rows"), 0, 0, tiled=True)
    up_loc = up_loc.reshape(dp_size * row_size * block_c, sub)
    down_loc = lax.all_to_all(w_down, "rows", 0, 1, tiled=True)
    down_loc = lax.all_gather(down_loc, "dp", axis=1, tiled=True)
    cotan = d_out.reshape(cells, width).astype(jnp.float32)
    back = (cotan * layer_scale).astype(jnp.bfloat16)
    rimmed = padded_2(feature_maps, (("rows", 1),), 3)
    padded = jnp.pad(rimmed.astype(jnp.float32), ((0, 0), (0, 0), (3, 3), (0, 0)))
    filtered = jnp.zeros(feature_maps.shape, jnp.float32)
    for row_off in range(KS):
        for col_off in range(KS):
            filtered = (
                filtered
                + padded[:, row_off : row_off + strip, col_off : col_off + across, :]
                * dw_kernel[row_off, col_off]
            )
    flat = filtered.reshape(cells, width)
    average = jnp.mean(flat, axis=-1, keepdims=True)
    center = flat - average
    variance = jnp.mean(center * center, axis=-1, keepdims=True)
    rstd = lax.rsqrt(variance + norm_eps)
    normed = center * rstd
    scaled = (normed * norm_gain).astype(jnp.bfloat16)
    pair = lax.all_gather(jnp.stack([scaled, back]), hid_axes, axis=1, tiled=True)
    gathered, back_all = (pair[0], pair[1])
    hidden = jnp.dot(gathered, up_loc, preferred_element_type=jnp.float32)
    active = gelu_exact(hidden).astype(jnp.bfloat16)
    mlp_terms = jnp.dot(active, down_loc, preferred_element_type=jnp.float32)
    down_part_t = lax.dot_general(
        back_all, active, contract_rows, preferred_element_type=jnp.float32
    )
    slope_in = lax.dot_general(
        back_all, down_loc, contract_cols, preferred_element_type=jnp.float32
    )
    hidden_grad = (slope_in * gelu_slope(hidden)).astype(jnp.bfloat16)
    up_part = lax.dot_general(
        gathered, hidden_grad, contract_rows, preferred_element_type=jnp.float32
    )
    norm_terms = lax.dot_general(
        hidden_grad, up_loc, contract_cols, preferred_element_type=jnp.float32
    )
    sums = lax.psum_scatter(
        jnp.stack([mlp_terms, norm_terms]).astype(jnp.bfloat16),
        hid_axes,
        scatter_dimension=1,
        tiled=True,
    ).astype(jnp.float32)
    branch, norm_grad = (sums[0], sums[1])
    resid = feature_maps.reshape(cells, width).astype(jnp.float32)
    result = (resid + layer_scale * branch).astype(jnp.bfloat16).reshape(feature_maps.shape)
    scale_part = jnp.sum(cotan * branch, axis=0)
    down_blocks = down_part_t.astype(jnp.bfloat16).reshape(dp_size, -1, sub)
    down_sum = lax.all_to_all(down_blocks, "dp", 0, 0, tiled=True).astype(jnp.float32).sum(0)
    up_sum = lax.psum_scatter(up_part.astype(jnp.bfloat16), "dp", scatter_dimension=0, tiled=True)
    grad_sums = jnp.stack([up_sum, down_sum.astype(jnp.bfloat16)])
    gain_part = jnp.sum(norm_grad * normed, axis=0)
    scaled_grad = norm_grad * norm_gain
    conv_grad = rstd * (
        scaled_grad
        - jnp.mean(scaled_grad, axis=-1, keepdims=True)
        - normed * jnp.mean(scaled_grad * normed, axis=-1, keepdims=True)
    )
    conv_grad = conv_grad.reshape(feature_maps.shape)
    grad_rim = padded_2(conv_grad.astype(jnp.bfloat16), (("rows", 1),), 3).astype(conv_grad.dtype)
    grad_pad = jnp.pad(grad_rim, ((0, 0), (0, 0), (3, 3), (0, 0)))
    kernel_rows = []
    back_conv = jnp.zeros(feature_maps.shape, jnp.float32)
    for row_off in range(KS):
        for col_off in range(KS):
            window = padded[:, row_off : row_off + strip, col_off : col_off + across, :]
            kernel_rows.append(jnp.sum(window * conv_grad, axis=(0, 1, 2)))
            back_conv = (
                back_conv
                + grad_pad[
                    :, 6 - row_off : 6 - row_off + strip, 6 - col_off : 6 - col_off + across, :
                ]
                * dw_kernel[row_off, col_off]
            )
    kernel_part = jnp.stack(kernel_rows).reshape(KS, KS, width)
    grad_x = (d_out.astype(jnp.float32) + back_conv).astype(jnp.bfloat16)
    grad_kernel, grad_gain, grad_scale = small_sums(kernel_part, gain_part, scale_part, width)
    grad_sums, grad_x, grad_kernel, grad_gain, grad_scale = lax.optimization_barrier(
        (grad_sums, grad_x, grad_kernel, grad_gain, grad_scale)
    )
    grad_sums = lax.all_to_all(grad_sums, "rows", 1, 2, tiled=True).astype(jnp.float32)
    grad_up, grad_down = (grad_sums[0], grad_sums[1].T)
    return (result, grad_x, grad_up, grad_down, grad_kernel, grad_gain, grad_scale)


def solution(mesh):
    return jax.shard_map(
        body,
        mesh=mesh,
        in_specs=(
            P(("dp", "fsdp"), "rows", None, None),
            P(),
            P(),
            P(("dp", "rows"), "fsdp"),
            P("fsdp", ("dp", "rows")),
            P(),
            P(("dp", "fsdp"), "rows", None, None),
        ),
        out_specs=(
            P(("dp", "fsdp"), "rows", None, None),
            P(("dp", "fsdp"), "rows", None, None),
            P(("dp", "rows"), "fsdp"),
            P("fsdp", ("dp", "rows")),
            P(),
            P(),
            P(),
        ),
        check_vma=False,
    )
```

profile of v0, /device:TPU:0, one launch (start us, length us, event | category | flops | bytes accessed | tf_op | source)
XLA Modules:
  0.0 350.1 jit_solution(6042365886521894993)
XLA Ops:
  7.2 1.1 fusion.114
  8.3 2.4 collective-permute-start
  10.7 1.3 collective-permute-start.1
  12.0 1.4 slice_reduce_fusion.48
  13.5 1.8 slice_reduce_fusion.50
  15.4 2.5 slice_reduce_fusion.49
  18.0 1.1 maximum_convert_fusion
  19.2 9.4 %fusion.110 = (f32[4,32]{1,0:T(4,128)S(1)}, f32[1,4,32,1536]{3,2,1,0:T(8,128)S(1)}) fusion(f32[1536]{0:T(1024)S(1)} %get-tuple-element.119, f32[1536]{0:T(1024)S(1)} %get-tuple-element.120, f32[1536]{0:T(1024)S(1)} %get-tuple-element.73, f32[1536]{0:T(1024)S(1)} %get-tuple-element.74, f32[1,10,32,1536]{3,2,1,0:T(8,128)S(1)} %maximum_convert_fusion, ...), kind=kLoop, calls=%fused_computation.332 | loop fusion | flops 19267456 | bytes 8641024 | tf_op jit(solution)/shard_map/reduce_sum | solution.py:80
  29.8 0.9 pad_maximum_fusion.2
  31.0 0.9 copy.45
  31.9 6.1 %all-to-all-start.1 = ((bf16[4,768,96]{1,2,0:T(8,128)(2,1)}), bf16[4,768,96]{1,2,0:T(8,128)(2,1)S(1)}, u32[]{:S(2)}, u32[]{:S(2)}) async-start(bf16[4,768,96]{1,2,0:T(8,128)(2,1)} %bitcast.94), calls=%async_computation.1 | async-start | bytes 1179648 | tf_op jit(solution)/shard_map/all_to_all | solution.py:65
  38.0 2.5 reshape.558
  40.5 2.0 copy.34
  42.5 7.0 %all-to-all-done.1 = bf16[4,768,96]{1,2,0:T(8,128)(2,1)S(1)} async-done(((bf16[4,768,96]{1,2,0:T(8,128)(2,1)}), bf16[4,768,96]{1,2,0:T(8,128)(2,1)S(1)}, u32[]{:S(2)}, u32[]{:S(2)}) %all-to-all-start.1) | async-done | bytes 589856 | tf_op jit(solution)/shard_map/all_to_all | solution.py:65
  49.5 2.9 broadcast_in_dim.8
  52.4 5.3 %all-to-all-start = ((bf16[16,96,768]{2,1,0:T(8,128)(2,1)}), bf16[16,96,768]{2,1,0:T(8,128)(2,1)}, u32[]{:S(2)}, u32[]{:S(2)}) async-start(bf16[16,96,768]{2,1,0:T(8,128)(2,1)} %bitcast.86), calls=%async_computation | async-start | bytes 4718592 | tf_op jit(solution)/shard_map/all_to_all | solution.py:63
  57.8 0.7 all-gather.5.cloned.1.call-update
  58.8 44.8 %all-to-all-done = bf16[16,96,768]{2,1,0:T(8,128)(2,1)} async-done(((bf16[16,96,768]{2,1,0:T(8,128)(2,1)}), bf16[16,96,768]{2,1,0:T(8,128)(2,1)}, u32[]{:S(2)}, u32[]{:S(2)}) %all-to-all-start) | async-done | bytes 2359328 | tf_op jit(solution)/shard_map/all_to_all | solution.py:63
  103.6 7.5 %multiply_convert_fusion = (bf16[1024,768]{1,0:T(8,128)(2,1)}, f32[1024,768]{1,0:T(8,128)}) fusion(bf16[1536,768]{1,0:T(8,128)(2,1)} %bitcast.5, bf16[2,1024,1536]{2,1,0:T(8,128)(2,1)} %all-gather.3.cloned.1.call-done), kind=kOutput, calls=%fused_computation.100 | convolution fusion | flops 2419851264 | bytes 10223616 | tf_op jit(solution)/shard_map/dot_general | solution.py:88
  111.1 43.2 %all-gather.5.cloned.1.call-done = bf16[768,1536]{0,1:T(8,128)(2,1)} async-done(((bf16[768,384]{0,1:T(8,128)(2,1)}), bf16[768,1536]{0,1:T(8,128)(2,1)}) %all-gather.5.cloned.1.call-update) | async-done | bytes 2359312 | tf_op jit(solution)/shard_map/all_gather | solution.py:66
  154.3 6.6 %fusion.7 = bf16[1024,768]{1,0:T(8,128)(2,1)S(1)} fusion(f32[1024,768]{1,0:T(8,128)} %get-tuple-element.134, bf16[768,1536]{0,1:T(8,128)(2,1)} %all-gather.5.cloned.1.call-done, bf16[2,1024,1536]{2,1,0:T(8,128)(2,1)} %all-gather.3.cloned.1.call-done), kind=kOutput, calls=%fused_computation.97 | convolution fusion | flops 2423783424 | bytes 10223616 | tf_op jit(solution)/shard_map/dot_general | solution.py:94
  161.0 5.1 %fusion.1 = bf16[1,1024,1536]{2,1,0:T(8,128)(2,1)S(1)} fusion(bf16[1024,768]{1,0:T(8,128)(2,1)S(1)} %fusion.7, bf16[1536,768]{1,0:T(8,128)(2,1)} %bitcast.5), kind=kOutput, calls=%fused_computation.91 | convolution fusion | flops 2417491968 | bytes 7077888 | tf_op jit(solution)/shard_map/dot_general | solution.py:101
  166.1 2.9 fusion
  169.1 3.2 pad_maximum_fusion
  172.8 6.5 %convolution_convert_fusion.3 = bf16[1536,768]{1,0:T(8,128)(2,1)} fusion(bf16[1024,768]{1,0:T(8,128)(2,1)} %copy-done.61, bf16[2,1024,1536]{2,1,0:T(8,128)(2,1)} %all-gather.3.cloned.1.call-done), kind=kOutput, calls=%fused_computation.89 | convolution fusion | flops 2417098752 | bytes 7077888 | tf_op jit(solution)/shard_map/dot_general | solution.py:98
  179.3 7.1 %convolution_convert_fusion.2 = bf16[1536,768]{1,0:T(8,128)(2,1)} fusion(bf16[1024,768]{1,0:T(8,128)(2,1)} %get-tuple-element.133, bf16[2,1024,1536]{2,1,0:T(8,128)(2,1)} %all-gather.3.cloned.1.call-done), kind=kOutput, calls=%fused_computation.88 | convolution fusion | flops 2417098752 | bytes 7077888 | tf_op jit(solution)/shard_map/dot_general | solution.py:91
  186.4 4.5 %all-to-all-start.2 = ((bf16[4,384,768]{2,1,0:T(8,128)(2,1)}), bf16[4,384,768]{2,1,0:T(8,128)(2,1)}, u32[]{:S(2)}, u32[]{:S(2)}) async-start(bf16[4,384,768]{2,1,0:T(8,128)(2,1)} %bitcast.92), calls=%async_computation.4 | async-start | bytes 4718592 | tf_op jit(solution)/shard_map/all_to_all | solution.py:115
  190.9 42.1 %reduce-scatter.3.cloned.1.call-done = bf16[2,128,1536]{2,1,0:T(8,128)(2,1)} async-done(((bf16[2,1024,1536]{2,1,0:T(8,128)(2,1)}), bf16[2,128,1536]{2,1,0:T(8,128)(2,1)}) %reduce-scatter.3.cloned.1.call-update) | async-done | bytes 786448 | tf_op jit(solution)/shard_map/reduce_scatter | solution.py:104
  233.0 1.4 convert_element_type.120
  234.4 2.1 fusion.104
  237.6 1.3 div.22
  238.9 1.2 broadcast_multiply_fusion.1
  240.1 1.3 div.24
  241.4 1.3 broadcast_in_dim.10
  242.7 1.0 fusion.112
  243.7 2.4 multiply_reduce_fusion
  246.3 2.0 multiply_reduce_fusion.18
  248.4 1.4 multiply_reduce_fusion.36
  250.8 1.0 reshape.563
  251.8 4.7 %all-to-all-start.3 = ((f32[32,2,1536]{2,1,0:T(2,128)}), f32[32,2,1536]{2,1,0:T(2,128)}, u32[]{:S(2)}, u32[]{:S(2)}) async-start(f32[32,2,1536]{2,1,0:T(2,128)} %reshape.563), calls=%async_computation.5 | async-start | bytes 786432 | tf_op jit(solution)/shard_map/all_to_all | solution.py:46
  256.6 2.1 collective-permute-start.2
  258.7 1.5 collective-permute-start.3
  260.2 2.3 reduce_sum.518
  262.5 27.8 %reduce-scatter.5.cloned.1.call-done = bf16[384,768]{1,0:T(8,128)(2,1)} async-done(((bf16[1536,768]{1,0:T(8,128)(2,1)}), bf16[384,768]{1,0:T(8,128)(2,1)}) %reduce-scatter.5.cloned.1.call-update) | async-done | bytes 589840 | tf_op jit(solution)/shard_map/reduce_scatter | solution.py:116
  290.2 1.2 pad_maximum_fusion.1
  291.5 0.7 copy-done.5
  292.2 1.2 maximum_convert_fusion.1
  293.4 1.1 reduce_sum.572
  294.5 0.8 broadcast_in_dim.11
  295.3 4.9 %all-to-all-start.4 = ((f32[32,2,1536]{2,1,0:T(2,128)}), f32[32,2,1536]{2,1,0:T(2,128)S(1)}, u32[]{:S(2)}, u32[]{:S(2)}) async-start(f32[32,2,1536]{2,1,0:T(2,128)} %broadcast_in_dim.11), calls=%async_computation.6 | async-start | bytes 786432 | tf_op jit(solution)/shard_map/all_to_all | solution.py:48
  300.3 8.3 %fusion.97 = bf16[1,4,32,1536]{3,2,1,0:T(8,128)(2,1)} fusion(f32[1,10,32,1536]{3,2,1,0:T(8,128)S(1)} %maximum_convert_fusion.1, f32[1536]{0:T(1024)} %copy-done.16, f32[1536]{0:T(1024)} %copy-done.17, f32[1536]{0:T(1024)} %copy-done.19, f32[1536]{0:T(1024)} %copy-done.20, f32[1536]{0:T(1024)} %copy-done.21, f32[1536]{0:T(1024)} %copy-done.22, ...), kind=kLoop, calls=%fused_computation.195 | loop fusion | flops 19660800 | bytes 8562688 | tf_op jit(solution)/shard_map/convert_element_type | solution.py:142
  308.6 4.8 %all-to-all-done.4 = f32[32,2,1536]{2,1,0:T(2,128)S(1)} async-done(((f32[32,2,1536]{2,1,0:T(2,128)}), f32[32,2,1536]{2,1,0:T(2,128)S(1)}, u32[]{:S(2)}, u32[]{:S(2)}) %all-to-all-start.4) | async-done | bytes 393248 | tf_op jit(solution)/shard_map/all_to_all | solution.py:48
  313.8 0.6 slice_reduce_fusion
  314.4 0.8 reshape.565
  315.2 2.2 copy.37
  317.4 3.5 %all-to-all-start.5 = ((bf16[2,384,768]{2,0,1:T(2,128)(2,1)}), bf16[2,384,768]{2,0,1:T(2,128)(2,1)S(1)}, u32[]{:S(2)}, u32[]{:S(2)}) async-start(bf16[2,384,768]{2,0,1:T(2,128)(2,1)} %copy.37), calls=%async_computation.7 | async-start | bytes 2359296 | tf_op jit(solution)/shard_map/all_to_all | solution.py:147
  321.0 2.0 add_convert_fusion
  322.9 13.8 %all-to-all-done.5 = bf16[2,384,768]{2,0,1:T(2,128)(2,1)S(1)} async-done(((bf16[2,384,768]{2,0,1:T(2,128)(2,1)}), bf16[2,384,768]{2,0,1:T(2,128)(2,1)S(1)}, u32[]{:S(2)}, u32[]{:S(2)}) %all-to-all-start.5) | async-done | bytes 1179680 | tf_op jit(solution)/shard_map/all_to_all | solution.py:147
  336.8 0.8 convert_bitcast_fusion
  337.6 1.8 fusion.111
  339.4 0.8 copy.39
  340.2 1.2 copy.43
  341.4 0.8 copy.38
  342.2 1.2 copy.42
  (199 shorter events, 4.4 us)
Async XLA Ops:
  7.2 96.4 %all-gather.3.cloned.1.call-start = ((), (), s32[]{:S(2)}) async-start(), calls=%async_computation.8 | async-start | bytes 7077888 | tf_op jit(solution)/shard_map/all_gather | solution.py:86
  8.3 9.7 %collective-permute-start = (bf16[1,3,32,1536]{3,2,1,0:T(8,128)(2,1)S(1)}, bf16[1,3,32,1536]{3,2,1,0:T(8,128)(2,1)S(1)}, u32[]{:S(2)}, u32[]{:S(2)}) collective-permute-start(bf16[1,3,32,1536]{3,2,1,0:T(8,128)(2,1)S(1)} %get-tuple-element.131), channel_id=1, source_target_pairs={{0,1},{1,2},{2,3},{4,5},{5,6},{6,7},{8,9},{9,10},{10,11},{12,13},{... | collective-permute-start | bytes 884744 | tf_op jit(solution)/shard_map/ppermute | solution.py:22
  10.7 7.3 %collective-permute-start.1 = (bf16[1,3,32,1536]{3,2,1,0:T(8,128)(2,1)S(1)}, bf16[1,3,32,1536]{3,2,1,0:T(8,128)(2,1)S(1)}, u32[]{:S(2)}, u32[]{:S(2)}) collective-permute-start(bf16[1,3,32,1536]{3,2,1,0:T(8,128)(2,1)S(1)} %get-tuple-element.132), channel_id=1, source_target_pairs={{1,0},{2,1},{3,2},{5,4},{6,5},{7,6},{9,8},{10,9},{11,10},{13,12},{... | collective-permute-start | bytes 884744 | tf_op jit(solution)/shard_map/ppermute | solution.py:23
  13.4 15.3 %copy-start.7 = (f32[1536]{0:T(1024)}, f32[1536]{0:T(1024)S(1)}, u32[]{:S(2)}) copy-start(f32[1536]{0:T(1024)S(1)} %get-tuple-element.111) | copy-start | bytes 18436
  13.4 15.3 %copy-start.9 = (f32[1536]{0:T(1024)}, f32[1536]{0:T(1024)S(1)}, u32[]{:S(2)}) copy-start(f32[1536]{0:T(1024)S(1)} %get-tuple-element.112) | copy-start | bytes 18436
  13.4 15.3 %copy-start.10 = (f32[1536]{0:T(1024)}, f32[1536]{0:T(1024)S(1)}, u32[]{:S(2)}) copy-start(f32[1536]{0:T(1024)S(1)} %get-tuple-element.113) | copy-start | bytes 18436
  13.4 15.3 %copy-start.11 = (f32[1536]{0:T(1024)}, f32[1536]{0:T(1024)S(1)}, u32[]{:S(2)}) copy-start(f32[1536]{0:T(1024)S(1)} %get-tuple-element.114) | copy-start | bytes 18436
  13.4 15.3 %copy-start.12 = (f32[1536]{0:T(1024)}, f32[1536]{0:T(1024)S(1)}, u32[]{:S(2)}) copy-start(f32[1536]{0:T(1024)S(1)} %get-tuple-element.115) | copy-start | bytes 18436
  13.4 15.3 %copy-start.13 = (f32[1536]{0:T(1024)}, f32[1536]{0:T(1024)S(1)}, u32[]{:S(2)}) copy-start(f32[1536]{0:T(1024)S(1)} %get-tuple-element.116) | copy-start | bytes 18436
  13.4 15.3 %copy-start.14 = (f32[1536]{0:T(1024)}, f32[1536]{0:T(1024)S(1)}, u32[]{:S(2)}) copy-start(f32[1536]{0:T(1024)S(1)} %get-tuple-element.117) | copy-start | bytes 18436
  13.4 15.3 %copy-start.15 = (f32[1536]{0:T(1024)}, f32[1536]{0:T(1024)S(1)}, u32[]{:S(2)}) copy-start(f32[1536]{0:T(1024)S(1)} %get-tuple-element.118) | copy-start | bytes 18436
  13.5 15.3 %copy-start.16 = (f32[1536]{0:T(1024)}, f32[1536]{0:T(1024)S(1)}, u32[]{:S(2)}) copy-start(f32[1536]{0:T(1024)S(1)} %get-tuple-element.119) | copy-start | bytes 18436
  13.5 15.3 %copy-start.17 = (f32[1536]{0:T(1024)}, f32[1536]{0:T(1024)S(1)}, u32[]{:S(2)}) copy-start(f32[1536]{0:T(1024)S(1)} %get-tuple-element.120) | copy-start | bytes 18436
  15.2 13.5 %copy-start.18 = (f32[1536]{0:T(1024)}, f32[1536]{0:T(1024)S(1)}, u32[]{:S(2)}) copy-start(f32[1536]{0:T(1024)S(1)} %get-tuple-element.72) | copy-start | bytes 18436
  15.3 13.5 %copy-start.19 = (f32[1536]{0:T(1024)}, f32[1536]{0:T(1024)S(1)}, u32[]{:S(2)}) copy-start(f32[1536]{0:T(1024)S(1)} %get-tuple-element.73) | copy-start | bytes 18436
  15.3 13.5 %copy-start.20 = (f32[1536]{0:T(1024)}, f32[1536]{0:T(1024)S(1)}, u32[]{:S(2)}) copy-start(f32[1536]{0:T(1024)S(1)} %get-tuple-element.74) | copy-start | bytes 18436
  15.3 13.5 %copy-start.21 = (f32[1536]{0:T(1024)}, f32[1536]{0:T(1024)S(1)}, u32[]{:S(2)}) copy-start(f32[1536]{0:T(1024)S(1)} %get-tuple-element.75) | copy-start | bytes 18436
  15.3 13.5 %copy-start.22 = (f32[1536]{0:T(1024)}, f32[1536]{0:T(1024)S(1)}, u32[]{:S(2)}) copy-start(f32[1536]{0:T(1024)S(1)} %get-tuple-element.76) | copy-start | bytes 18436
  15.3 13.5 %copy-start.23 = (f32[1536]{0:T(1024)}, f32[1536]{0:T(1024)S(1)}, u32[]{:S(2)}) copy-start(f32[1536]{0:T(1024)S(1)} %get-tuple-element.77) | copy-start | bytes 18436
  15.3 13.5 %copy-start.24 = (f32[1536]{0:T(1024)}, f32[1536]{0:T(1024)S(1)}, u32[]{:S(2)}) copy-start(f32[1536]{0:T(1024)S(1)} %get-tuple-element.78) | copy-start | bytes 18436
  15.3 13.5 %copy-start.25 = (f32[1536]{0:T(1024)}, f32[1536]{0:T(1024)S(1)}, u32[]{:S(2)}) copy-start(f32[1536]{0:T(1024)S(1)} %get-tuple-element.79) | copy-start | bytes 18436
  15.3 13.5 %copy-start.26 = (f32[1536]{0:T(1024)}, f32[1536]{0:T(1024)S(1)}, u32[]{:S(2)}) copy-start(f32[1536]{0:T(1024)S(1)} %get-tuple-element.80) | copy-start | bytes 18436
  15.3 13.5 %copy-start.27 = (f32[1536]{0:T(1024)}, f32[1536]{0:T(1024)S(1)}, u32[]{:S(2)}) copy-start(f32[1536]{0:T(1024)S(1)} %get-tuple-element.81) | copy-start | bytes 18436
  15.3 13.5 %copy-start.28 = (f32[1536]{0:T(1024)}, f32[1536]{0:T(1024)S(1)}, u32[]{:S(2)}) copy-start(f32[1536]{0:T(1024)S(1)} %get-tuple-element.82) | copy-start | bytes 18436
  15.4 13.5 %copy-start.29 = (f32[1536]{0:T(1024)}, f32[1536]{0:T(1024)S(1)}, u32[]{:S(2)}) copy-start(f32[1536]{0:T(1024)S(1)} %get-tuple-element.83) | copy-start | bytes 18436
  15.4 13.5 %copy-start.30 = (f32[1536]{0:T(1024)}, f32[1536]{0:T(1024)S(1)}, u32[]{:S(2)}) copy-start(f32[1536]{0:T(1024)S(1)} %get-tuple-element.84) | copy-start | bytes 18436
  15.4 13.5 %copy-start.31 = (f32[1536]{0:T(1024)}, f32[1536]{0:T(1024)S(1)}, u32[]{:S(2)}) copy-start(f32[1536]{0:T(1024)S(1)} %get-tuple-element.85) | copy-start | bytes 18436
  15.4 13.5 %copy-start.32 = (f32[1536]{0:T(1024)}, f32[1536]{0:T(1024)S(1)}, u32[]{:S(2)}) copy-start(f32[1536]{0:T(1024)S(1)} %get-tuple-element.86) | copy-start | bytes 18436
  15.4 13.5 %copy-start.33 = (f32[1536]{0:T(1024)}, f32[1536]{0:T(1024)S(1)}, u32[]{:S(2)}) copy-start(f32[1536]{0:T(1024)S(1)} %get-tuple-element.87) | copy-start | bytes 18436
  15.4 13.5 %copy-start.34 = (f32[1536]{0:T(1024)}, f32[1536]{0:T(1024)S(1)}, u32[]{:S(2)}) copy-start(f32[1536]{0:T(1024)S(1)} %get-tuple-element.88) | copy-start | bytes 18436
  15.4 13.5 %copy-start.35 = (f32[1536]{0:T(1024)}, f32[1536]{0:T(1024)S(1)}, u32[]{:S(2)}) copy-start(f32[1536]{0:T(1024)S(1)} %get-tuple-element.89) | copy-start | bytes 18436
  15.4 13.5 %copy-start.36 = (f32[1536]{0:T(1024)}, f32[1536]{0:T(1024)S(1)}, u32[]{:S(2)}) copy-start(f32[1536]{0:T(1024)S(1)} %get-tuple-element.90) | copy-start | bytes 18436
  17.9 11.0 %copy-start.37 = (f32[1536]{0:T(1024)}, f32[1536]{0:T(1024)S(1)}, u32[]{:S(2)}) copy-start(f32[1536]{0:T(1024)S(1)} %get-tuple-element.91) | copy-start | bytes 18436
  17.9 11.0 %copy-start.38 = (f32[1536]{0:T(1024)}, f32[1536]{0:T(1024)S(1)}, u32[]{:S(2)}) copy-start(f32[1536]{0:T(1024)S(1)} %get-tuple-element.92) | copy-start | bytes 18436
  17.9 11.0 %copy-start.39 = (f32[1536]{0:T(1024)}, f32[1536]{0:T(1024)S(1)}, u32[]{:S(2)}) copy-start(f32[1536]{0:T(1024)S(1)} %get-tuple-element.93) | copy-start | bytes 18436
  17.9 11.0 %copy-start.40 = (f32[1536]{0:T(1024)}, f32[1536]{0:T(1024)S(1)}, u32[]{:S(2)}) copy-start(f32[1536]{0:T(1024)S(1)} %get-tuple-element.94) | copy-start | bytes 18436
  18.0 11.0 %copy-start.41 = (f32[1536]{0:T(1024)}, f32[1536]{0:T(1024)S(1)}, u32[]{:S(2)}) copy-start(f32[1536]{0:T(1024)S(1)} %get-tuple-element.95) | copy-start | bytes 18436
  18.0 11.0 %copy-start.42 = (f32[1536]{0:T(1024)}, f32[1536]{0:T(1024)S(1)}, u32[]{:S(2)}) copy-start(f32[1536]{0:T(1024)S(1)} %get-tuple-element.96) | copy-start | bytes 18436
  18.0 11.0 %copy-start.43 = (f32[1536]{0:T(1024)}, f32[1536]{0:T(1024)S(1)}, u32[]{:S(2)}) copy-start(f32[1536]{0:T(1024)S(1)} %get-tuple-element.97) | copy-start | bytes 18436
  18.0 11.0 %copy-start.44 = (f32[1536]{0:T(1024)}, f32[1536]{0:T(1024)S(1)}, u32[]{:S(2)}) copy-start(f32[1536]{0:T(1024)S(1)} %get-tuple-element.98) | copy-start | bytes 18436
  18.0 11.0 %copy-start.45 = (f32[1536]{0:T(1024)}, f32[1536]{0:T(1024)S(1)}, u32[]{:S(2)}) copy-start(f32[1536]{0:T(1024)S(1)} %get-tuple-element.99) | copy-start | bytes 18436
  18.0 11.0 %copy-start.46 = (f32[1536]{0:T(1024)}, f32[1536]{0:T(1024)S(1)}, u32[]{:S(2)}) copy-start(f32[1536]{0:T(1024)S(1)} %get-tuple-element.100) | copy-start | bytes 18436
  19.2 10.3 %copy-start.2 = (bf16[1,4,32,1536]{3,2,1,0:T(8,128)(2,1)S(1)}, bf16[1,4,32,1536]{3,2,1,0:T(8,128)(2,1)}, u32[]{:S(2)}) copy-start(bf16[1,4,32,1536]{3,2,1,0:T(8,128)(2,1)} %param.13) | copy-start | bytes 1179652
  19.2 10.3 %copy-start.6 = (f32[1536]{0:T(1024)S(1)}, f32[1536]{0:T(1024)}, u32[]{:S(2)}) copy-start(f32[1536]{0:T(1024)} %param.9) | copy-start | bytes 18436
  19.2 10.3 %copy-start.47 = (f32[1536]{0:T(1024)S(1)}, f32[1536]{0:T(1024)}, u32[]{:S(2)}) copy-start(f32[1536]{0:T(1024)} %param.12) | copy-start | bytes 18436
  31.9 17.6 %all-to-all-start.1 = ((bf16[4,768,96]{1,2,0:T(8,128)(2,1)}), bf16[4,768,96]{1,2,0:T(8,128)(2,1)S(1)}, u32[]{:S(2)}, u32[]{:S(2)}) async-start(bf16[4,768,96]{1,2,0:T(8,128)(2,1)} %bitcast.94), calls=%async_computation.1 | async-start | bytes 1179648 | tf_op jit(solution)/shard_map/all_to_all | solution.py:65
  49.5 2.9 copy-start.3
  52.4 51.2 %all-to-all-start = ((bf16[16,96,768]{2,1,0:T(8,128)(2,1)}), bf16[16,96,768]{2,1,0:T(8,128)(2,1)}, u32[]{:S(2)}, u32[]{:S(2)}) async-start(bf16[16,96,768]{2,1,0:T(8,128)(2,1)} %bitcast.86), calls=%async_computation | async-start | bytes 4718592 | tf_op jit(solution)/shard_map/all_to_all | solution.py:63
  57.7 96.6 %all-gather.5.cloned.1.call-start = ((), (), s32[]{:S(2)}) async-start(), calls=%async_computation.9 | async-start | bytes 2949120 | tf_op jit(solution)/shard_map/all_gather | solution.py:66
  58.5 174.5 %reduce-scatter.3.cloned.1.call-start = ((), (), s32[]{:S(2)}) async-start(), calls=%async_computation.10 | async-start | bytes 7077888 | tf_op jit(solution)/shard_map/reduce_scatter | solution.py:104
  160.9 5.2 %copy-start.61 = (bf16[1024,768]{1,0:T(8,128)(2,1)}, bf16[1024,768]{1,0:T(8,128)(2,1)S(1)}, u32[]{:S(2)}) copy-start(bf16[1024,768]{1,0:T(8,128)(2,1)S(1)} %fusion.7) | copy-start | bytes 4718596
  161.0 5.2 %copy-start.59 = (bf16[768,1536]{0,1:T(8,128)(2,1)S(1)}, bf16[768,1536]{0,1:T(8,128)(2,1)}, u32[]{:S(2)}) copy-start(bf16[768,1536]{0,1:T(8,128)(2,1)} %all-gather.5.cloned.1.call-done) | copy-start | bytes 7077892
  161.0 5.2 %copy-start.60 = (bf16[1024,768]{1,0:T(8,128)(2,1)S(1)}, bf16[1024,768]{1,0:T(8,128)(2,1)}, u32[]{:S(2)}) copy-start(bf16[1024,768]{1,0:T(8,128)(2,1)} %get-tuple-element.133) | copy-start | bytes 4718596
  172.3 118.0 %reduce-scatter.5.cloned.1.call-start = ((), (), s32[]{:S(2)}) async-start(), calls=%async_computation.11 | async-start | bytes 2949120 | tf_op jit(solution)/shard_map/reduce_scatter | solution.py:116
  186.4 65.4 %all-to-all-start.2 = ((bf16[4,384,768]{2,1,0:T(8,128)(2,1)}), bf16[4,384,768]{2,1,0:T(8,128)(2,1)}, u32[]{:S(2)}, u32[]{:S(2)}) async-start(bf16[4,384,768]{2,1,0:T(8,128)(2,1)} %bitcast.92), calls=%async_computation.4 | async-start | bytes 4718592 | tf_op jit(solution)/shard_map/all_to_all | solution.py:115
  233.0 9.7 %copy-start = (bf16[2,128,1536]{2,1,0:T(8,128)(2,1)S(1)}, bf16[2,128,1536]{2,1,0:T(8,128)(2,1)}, u32[]{:S(2)}) copy-start(bf16[2,128,1536]{2,1,0:T(8,128)(2,1)} %reduce-scatter.3.cloned.1.call-done) | copy-start | bytes 2359300
  251.8 41.5 %all-to-all-start.3 = ((f32[32,2,1536]{2,1,0:T(2,128)}), f32[32,2,1536]{2,1,0:T(2,128)}, u32[]{:S(2)}, u32[]{:S(2)}) async-start(f32[32,2,1536]{2,1,0:T(2,128)} %reshape.563), calls=%async_computation.5 | async-start | bytes 786432 | tf_op jit(solution)/shard_map/all_to_all | solution.py:46
  256.6 34.9 %collective-permute-start.2 = (bf16[1,3,32,1536]{3,2,1,0:T(8,128)(2,1)S(1)}, bf16[1,3,32,1536]{3,2,1,0:T(8,128)(2,1)S(1)}, u32[]{:S(2)}, u32[]{:S(2)}) collective-permute-start(bf16[1,3,32,1536]{3,2,1,0:T(8,128)(2,1)S(1)} %get-tuple-element.129), channel_id=1, source_target_pairs={{0,1},{1,2},{2,3},{4,5},{5,6},{6,7},{8,9},{9,10},{10,11},{12,13},{... | collective-permute-start | bytes 884744 | tf_op jit(solution)/shard_map/ppermute | solution.py:22
  258.7 33.5 %collective-permute-start.3 = (bf16[1,3,32,1536]{3,2,1,0:T(8,128)(2,1)S(1)}, bf16[1,3,32,1536]{3,2,1,0:T(8,128)(2,1)}, u32[]{:S(2)}, u32[]{:S(2)}) collective-permute-start(bf16[1,3,32,1536]{3,2,1,0:T(8,128)(2,1)S(1)} %get-tuple-element.130), channel_id=1, source_target_pairs={{1,0},{2,1},{3,2},{5,4},{6,5},{7,6},{9,8},{10,9},{11,10},{13,12},{... | collective-permute-start | bytes 884744 | tf_op jit(solution)/shard_map/ppermute | solution.py:23
  291.4 8.9 %copy-start.8 = (f32[1536]{0:T(1024)S(1)}, f32[1536]{0:T(1024)}, u32[]{:S(2)}) copy-start(f32[1536]{0:T(1024)} %copy-done.7) | copy-start | bytes 18436
  295.3 18.1 %all-to-all-start.4 = ((f32[32,2,1536]{2,1,0:T(2,128)}), f32[32,2,1536]{2,1,0:T(2,128)S(1)}, u32[]{:S(2)}, u32[]{:S(2)}) async-start(f32[32,2,1536]{2,1,0:T(2,128)} %broadcast_in_dim.11), calls=%async_computation.6 | async-start | bytes 786432 | tf_op jit(solution)/shard_map/all_to_all | solution.py:48
  315.2 5.8 %copy-start.1 = (bf16[1,4,32,1536]{3,2,1,0:T(8,128)(2,1)S(1)}, bf16[1,4,32,1536]{3,2,1,0:T(8,128)(2,1)}, u32[]{:S(2)}) copy-start(bf16[1,4,32,1536]{3,2,1,0:T(8,128)(2,1)} %param.7) | copy-start | bytes 1179652
  315.2 5.8 %copy-start.48 = (f32[1536]{0:T(1024)S(1)}, f32[1536]{0:T(1024)}, u32[]{:S(2)}) copy-start(f32[1536]{0:T(1024)} %param.12) | copy-start | bytes 18436
  317.4 19.4 %all-to-all-start.5 = ((bf16[2,384,768]{2,0,1:T(2,128)(2,1)}), bf16[2,384,768]{2,0,1:T(2,128)(2,1)S(1)}, u32[]{:S(2)}, u32[]{:S(2)}) async-start(bf16[2,384,768]{2,0,1:T(2,128)(2,1)} %copy.37), calls=%async_computation.7 | async-start | bytes 2359296 | tf_op jit(solution)/shard_map/all_to_all | solution.py:147
  (12 other events, 23.2 us)
Sparse Core Ops, SparseCore 0:
  30.9 67.5 all-gather.2
  100.6 53.6 all-gather.4
  172.4 60.5 reduce-scatter.2
  235.3 54.9 reduce-scatter.4
where the time goes:
time: 357 us; the launch traced here: 350 us
  waiting for transfers between devices  184 us (52%)
  other arithmetic  43 us (12%)
  starting transfers between devices  37.2 us (10%)
  matrix products  35.8 us (10%)
  local copies, waits for them, and re-layouts  34.4 us (10%)
  between operations  15.4 us (4%)
    all_to_all x1, waiting for transfers between devices, body(): up_loc = lax.all_to_all(pieces, ('dp', 'rows'), 0, 0, tiled=True)  44.8 us
    all_gather x1, waiting for transfers between devices, body(): down_loc = lax.all_gather(down_loc, 'dp', axis=1, tiled=True)  43.2 us
    reduce_scatter x1, waiting for transfers between devices, body(): lax.psum_scatter(jnp.stack([mlp_terms, norm_terms]).astype(jnp.bfloat16),...  42.1 us
    reduce_scatter x1, waiting for transfers between devices, body(): lax.psum_scatter(up_part.astype(jnp.bfloat16), 'dp', scatter_dimension=0,...  27.8 us
    all_to_all x1, waiting for transfers between devices, body(): lax.all_to_all(grad_sums, 'rows', 1, 2, tiled=True).astype(jnp.float32)  13.8 us
    reduce_sum x1, other arithmetic, body(): average = jnp.mean(flat, axis=-1, keepdims=True)  9.44 us
    convert_element_type x1, other arithmetic, body(): grad_x = (d_out.astype(jnp.float32) + back_conv).astype(jnp.bfloat16)  8.33 us
    dot_general x1, matrix products, body(): hidden = jnp.dot(gathered, up_loc, preferred_element_type=jnp.float32)  7.49 us
  transfers between devices with their start and end apart: 14, of which 7 were waited for; matrix products, arithmetic and copies ran while one was open for 20% of the time, Pallas kernels for 0%

commit v1 on v0

--- a/solution.py
+++ b/solution.py
@@ -3,6 +3,7 @@
 import jax.numpy as jnp
 from jax import lax
 from jax.sharding import PartitionSpec as P
+from jax.lax import axis_index, axis_size, ppermute
 
 KS = 7
 norm_eps = 1e-06
@@ -10,6 +11,18 @@
 inv_root_two_pi = 1.0 / math.sqrt(2.0 * math.pi)
 contract_rows = (((0,), (0,)), ((), ()))
 contract_cols = (((1,), (1,)), ((), ()))
+
+
+def draft_halves(s0, on_dim, v0):
+    now = s0.shape
+    extra = s0.reshape(*now[:on_dim], v0, now[on_dim] // v0, *now[on_dim + 1 :])
+    return jnp.moveaxis(extra, on_dim, 0)
+
+
+def use_the_results(xx, dim_at):
+    answer = list(xx.shape[1:])
+    answer[dim_at] *= xx.shape[0]
+    return jnp.moveaxis(xx, 0, dim_at).reshape(answer)
 
 
 def padded_2(x, sides, width):
@@ -144,7 +157,22 @@
     grad_sums, grad_x, grad_kernel, grad_gain, grad_scale = lax.optimization_barrier(
         (grad_sums, grad_x, grad_kernel, grad_gain, grad_scale)
     )
-    grad_sums = lax.all_to_all(grad_sums, "rows", 1, 2, tiled=True).astype(jnp.float32)
+
+    def unite_run_up(content, along_axis, page, z_in):
+        e_now, y1 = (axis_size(along_axis), axis_index(along_axis))
+        outer = draft_halves(content, page, e_now)
+        ledger = [outer[y1]]
+        for nth in tuple(range(1, e_now)):
+            aux = outer[(y1 + nth) % e_now]
+            ledger.append(
+                ppermute(
+                    aux, axis_name=along_axis, perm=[(u, (u + nth) % e_now) for u in range(e_now)]
+                )
+            )
+        outer = jnp.stack(ledger, axis=0)[(y1 - jnp.arange(e_now)) % e_now]
+        return use_the_results(outer, z_in)
+
+    grad_sums = unite_run_up(grad_sums, "rows", 1, 2).astype(jnp.float32)
     grad_up, grad_down = (grad_sums[0], grad_sums[1].T)
     return (result, grad_x, grad_up, grad_down, grad_kernel, grad_gain, grad_scale)
 

time: 357 us -> 343 us (0.961); the launches traced: 350 us -> 342 us
    all_to_all x1 -> x0, waiting for transfers between devices: 13.8 us -> none  [body(): lax.all_to_all(grad_sums, 'rows', 1, 2, tiled=True).astype(jnp.float32)]
    ppermute x0 -> x3, waiting for transfers between devices: none -> 13.3 us  [unite_run_up(): ppermute(aux, axis_name=along_axis, perm=[(u, (u + nth) % e_now) for u in...]
  transfers between devices with their start and end apart: 14 -> 16, of which waited for: 7 -> 9; matrix products, arithmetic and copies ran while one was open for 20% -> 20% of each run, Pallas kernels for 0% -> 0%
where the time goes in v1:
time: 343 us; the launch traced here: 342 us
  waiting for transfers between devices  183 us (53%)
  other arithmetic  42.1 us (12%)
  matrix products  35.8 us (10%)
  starting transfers between devices  34.4 us (10%)
  local copies, waits for them, and re-layouts  31.3 us (9%)
  between operations  15.3 us (4%)
    all_to_all x1, waiting for transfers between devices, body(): up_loc = lax.all_to_all(pieces, ('dp', 'rows'), 0, 0, tiled=True)  44.9 us
    all_gather x1, waiting for transfers between devices, body(): down_loc = lax.all_gather(down_loc, 'dp', axis=1, tiled=True)  43.2 us
    reduce_scatter x1, waiting for transfers between devices, body(): lax.psum_scatter(jnp.stack([mlp_terms, norm_terms]).astype(jnp.bfloat16),...  42.3 us
    reduce_scatter x1, waiting for transfers between devices, body(): lax.psum_scatter(up_part.astype(jnp.bfloat16), 'dp', scatter_dimension=0,...  26.9 us
    ppermute x3, waiting for transfers between devices, unite_run_up(): ppermute(aux, axis_name=along_axis, perm=[(u, (u + nth) % e_now) for u in...  13.3 us
    reduce_sum x1, other arithmetic, body(): average = jnp.mean(flat, axis=-1, keepdims=True)  9.44 us
    convert_element_type x1, other arithmetic, body(): grad_x = (d_out.astype(jnp.float32) + back_conv).astype(jnp.bfloat16)  8.33 us
    dot_general x1, matrix products, body(): hidden = jnp.dot(gathered, up_loc, preferred_element_type=jnp.float32)  7.49 us
  transfers between devices with their start and end apart: 16, of which 9 were waited for; matrix products, arithmetic and copies ran while one was open for 20% of the time, Pallas kernels for 0%

profile of v1, /device:TPU:0, one launch (start us, length us, event | category | flops | bytes accessed | tf_op | source)
XLA Modules:
  0.0 342.0 jit_solution(15026360710991722096)
XLA Ops:
  7.2 1.1 fusion.116
  8.3 2.4 collective-permute-start
  10.7 1.3 collective-permute-start.1
  12.0 1.4 slice_reduce_fusion.48
  13.5 1.8 slice_reduce_fusion.50
  15.6 2.4 slice_reduce_fusion.49
  18.1 1.1 maximum_convert_fusion
  19.2 9.4 %fusion.112 = (f32[4,32]{1,0:T(4,128)S(1)}, f32[1,4,32,1536]{3,2,1,0:T(8,128)S(1)}) fusion(f32[1536]{0:T(1024)S(1)} %get-tuple-element.119, f32[1536]{0:T(1024)S(1)} %get-tuple-element.120, f32[1536]{0:T(1024)S(1)} %get-tuple-element.73, f32[1536]{0:T(1024)S(1)} %get-tuple-element.74, f32[1,10,32,1536]{3,2,1,0:T(8,128)S(1)} %maximum_convert_fusion, ...), kind=kLoop, calls=%fused_computation.345 | loop fusion | flops 19267456 | bytes 8641024 | tf_op jit(solution)/shard_map/reduce_sum | solution.py:93
  29.8 0.9 pad_maximum_fusion.3
  31.1 0.9 copy.38
  31.9 6.1 %all-to-all-start.1 = ((bf16[4,768,96]{1,2,0:T(8,128)(2,1)}), bf16[4,768,96]{1,2,0:T(8,128)(2,1)S(1)}, u32[]{:S(2)}, u32[]{:S(2)}) async-start(bf16[4,768,96]{1,2,0:T(8,128)(2,1)} %bitcast.106), calls=%async_computation.1 | async-start | bytes 1179648 | tf_op jit(solution)/shard_map/all_to_all | solution.py:78
  38.1 2.5 reshape.616
  40.5 2.0 copy.28
  42.5 7.0 %all-to-all-done.1 = bf16[4,768,96]{1,2,0:T(8,128)(2,1)S(1)} async-done(((bf16[4,768,96]{1,2,0:T(8,128)(2,1)}), bf16[4,768,96]{1,2,0:T(8,128)(2,1)S(1)}, u32[]{:S(2)}, u32[]{:S(2)}) %all-to-all-start.1) | async-done | bytes 589856 | tf_op jit(solution)/shard_map/all_to_all | solution.py:78
  49.5 2.9 broadcast_in_dim.8
  52.4 5.3 %all-to-all-start = ((bf16[16,96,768]{2,1,0:T(8,128)(2,1)}), bf16[16,96,768]{2,1,0:T(8,128)(2,1)}, u32[]{:S(2)}, u32[]{:S(2)}) async-start(bf16[16,96,768]{2,1,0:T(8,128)(2,1)} %bitcast.98), calls=%async_computation | async-start | bytes 4718592 | tf_op jit(solution)/shard_map/all_to_all | solution.py:76
  57.8 0.7 all-gather.5.cloned.1.call-update
  58.7 44.9 %all-to-all-done = bf16[16,96,768]{2,1,0:T(8,128)(2,1)} async-done(((bf16[16,96,768]{2,1,0:T(8,128)(2,1)}), bf16[16,96,768]{2,1,0:T(8,128)(2,1)}, u32[]{:S(2)}, u32[]{:S(2)}) %all-to-all-start) | async-done | bytes 2359328 | tf_op jit(solution)/shard_map/all_to_all | solution.py:76
  103.6 7.5 %multiply_convert_fusion = (bf16[1024,768]{1,0:T(8,128)(2,1)}, f32[1024,768]{1,0:T(8,128)}) fusion(bf16[1536,768]{1,0:T(8,128)(2,1)} %bitcast.5, bf16[2,1024,1536]{2,1,0:T(8,128)(2,1)} %all-gather.3.cloned.1.call-done), kind=kOutput, calls=%fused_computation.101 | convolution fusion | flops 2419851264 | bytes 10223616 | tf_op jit(solution)/shard_map/dot_general | solution.py:101
  111.1 43.2 %all-gather.5.cloned.1.call-done = bf16[768,1536]{0,1:T(8,128)(2,1)} async-done(((bf16[768,384]{0,1:T(8,128)(2,1)}), bf16[768,1536]{0,1:T(8,128)(2,1)}) %all-gather.5.cloned.1.call-update) | async-done | bytes 2359312 | tf_op jit(solution)/shard_map/all_gather | solution.py:79
  154.3 6.6 %fusion.7 = bf16[1024,768]{1,0:T(8,128)(2,1)S(1)} fusion(f32[1024,768]{1,0:T(8,128)} %get-tuple-element.138, bf16[768,1536]{0,1:T(8,128)(2,1)} %all-gather.5.cloned.1.call-done, bf16[2,1024,1536]{2,1,0:T(8,128)(2,1)} %all-gather.3.cloned.1.call-done), kind=kOutput, calls=%fused_computation.98 | convolution fusion | flops 2423783424 | bytes 10223616 | tf_op jit(solution)/shard_map/dot_general | solution.py:107
  161.0 5.1 %fusion.1 = bf16[1,1024,1536]{2,1,0:T(8,128)(2,1)S(1)} fusion(bf16[1024,768]{1,0:T(8,128)(2,1)S(1)} %fusion.7, bf16[1536,768]{1,0:T(8,128)(2,1)} %bitcast.5), kind=kOutput, calls=%fused_computation.92 | convolution fusion | flops 2417491968 | bytes 7077888 | tf_op jit(solution)/shard_map/dot_general | solution.py:114
  166.2 2.9 fusion
  169.1 3.2 pad_maximum_fusion
  172.6 6.5 %convolution_convert_fusion.3 = bf16[1536,768]{1,0:T(8,128)(2,1)} fusion(bf16[1024,768]{1,0:T(8,128)(2,1)} %copy-done.62, bf16[2,1024,1536]{2,1,0:T(8,128)(2,1)} %all-gather.3.cloned.1.call-done), kind=kOutput, calls=%fused_computation.90 | convolution fusion | flops 2417098752 | bytes 7077888 | tf_op jit(solution)/shard_map/dot_general | solution.py:111
  179.1 7.2 %convolution_convert_fusion.2 = bf16[1536,768]{1,0:T(8,128)(2,1)} fusion(bf16[1024,768]{1,0:T(8,128)(2,1)} %get-tuple-element.137, bf16[2,1024,1536]{2,1,0:T(8,128)(2,1)} %all-gather.3.cloned.1.call-done), kind=kOutput, calls=%fused_computation.89 | convolution fusion | flops 2417098752 | bytes 7077888 | tf_op jit(solution)/shard_map/dot_general | solution.py:104
  186.2 4.5 %all-to-all-start.2 = ((bf16[4,384,768]{2,1,0:T(8,128)(2,1)}), bf16[4,384,768]{2,1,0:T(8,128)(2,1)}, u32[]{:S(2)}, u32[]{:S(2)}) async-start(bf16[4,384,768]{2,1,0:T(8,128)(2,1)} %bitcast.104), calls=%async_computation.4 | async-start | bytes 4718592 | tf_op jit(solution)/shard_map/all_to_all | solution.py:128
  190.7 42.3 %reduce-scatter.3.cloned.1.call-done = bf16[2,128,1536]{2,1,0:T(8,128)(2,1)} async-done(((bf16[2,1024,1536]{2,1,0:T(8,128)(2,1)}), bf16[2,128,1536]{2,1,0:T(8,128)(2,1)}) %reduce-scatter.3.cloned.1.call-update) | async-done | bytes 786448 | tf_op jit(solution)/shard_map/reduce_scatter | solution.py:117
  233.0 1.4 convert_element_type.117
  234.4 2.1 fusion.104
  236.5 0.6 broadcast_in_dim.9
  237.6 1.3 div.22
  238.9 1.2 broadcast_multiply_fusion.1
  240.1 1.3 div.24
  241.4 1.3 broadcast_in_dim.10
  242.7 1.0 fusion.114
  243.7 2.4 multiply_reduce_fusion
  246.4 2.0 multiply_reduce_fusion.18
  248.4 1.4 multiply_reduce_fusion.36
  250.9 1.0 reshape.621
  251.8 4.7 %all-to-all-start.3 = ((f32[32,2,1536]{2,1,0:T(2,128)}), f32[32,2,1536]{2,1,0:T(2,128)}, u32[]{:S(2)}, u32[]{:S(2)}) async-start(f32[32,2,1536]{2,1,0:T(2,128)} %reshape.621), calls=%async_computation.5 | async-start | bytes 786432 | tf_op jit(solution)/shard_map/all_to_all | solution.py:59
  256.6 2.1 collective-permute-start.2
  258.7 1.6 collective-permute-start.3
  260.9 2.3 reduce_sum.518
  263.2 26.9 %reduce-scatter.5.cloned.1.call-done = bf16[384,768]{1,0:T(8,128)(2,1)} async-done(((bf16[1536,768]{1,0:T(8,128)(2,1)}), bf16[384,768]{1,0:T(8,128)(2,1)}) %reduce-scatter.5.cloned.1.call-update) | async-done | bytes 589840 | tf_op jit(solution)/shard_map/reduce_scatter | solution.py:129
  290.1 1.2 pad_maximum_fusion.1
  291.3 0.7 copy-done.6
  292.0 1.2 maximum_convert_fusion.1
  293.3 1.1 reduce_sum.572
  294.4 0.8 broadcast_in_dim.11
  295.2 4.8 %all-to-all-start.4 = ((f32[32,2,1536]{2,1,0:T(2,128)}), f32[32,2,1536]{2,1,0:T(2,128)S(1)}, u32[]{:S(2)}, u32[]{:S(2)}) async-start(f32[32,2,1536]{2,1,0:T(2,128)} %broadcast_in_dim.11), calls=%async_computation.6 | async-start | bytes 786432 | tf_op jit(solution)/shard_map/all_to_all | solution.py:61
  300.0 8.3 %fusion.97 = bf16[1,4,32,1536]{3,2,1,0:T(8,128)(2,1)} fusion(f32[1,10,32,1536]{3,2,1,0:T(8,128)S(1)} %maximum_convert_fusion.1, f32[1536]{0:T(1024)} %copy-done.17, f32[1536]{0:T(1024)} %copy-done.18, f32[1536]{0:T(1024)} %copy-done.20, f32[1536]{0:T(1024)} %copy-done.21, f32[1536]{0:T(1024)} %copy-done.22, f32[1536]{0:T(1024)} %copy-done.23, ...), kind=kLoop, calls=%fused_computation.197 | loop fusion | flops 19660800 | bytes 8562688 | tf_op jit(solution)/shard_map/convert_element_type | solution.py:155
  308.4 4.8 %all-to-all-done.4 = f32[32,2,1536]{2,1,0:T(2,128)S(1)} async-done(((f32[32,2,1536]{2,1,0:T(2,128)}), f32[32,2,1536]{2,1,0:T(2,128)S(1)}, u32[]{:S(2)}, u32[]{:S(2)}) %all-to-all-start.4) | async-done | bytes 393248 | tf_op jit(solution)/shard_map/all_to_all | solution.py:61
  313.5 0.6 slice_reduce_fusion
  314.1 0.8 reshape.623
  315.0 0.6 collective-permute-start.6
  316.1 0.8 add_convert_fusion
  316.9 6.0 %collective-permute-done.6 = bf16[2,96,768]{2,1,0:T(8,128)(2,1)S(1)} collective-permute-done((bf16[2,96,768]{2,1,0:T(8,128)(2,1)S(1)}, bf16[2,96,768]{2,1,0:T(8,128)(2,1)S(1)}, u32[]{:S(2)}, u32[]{:S(2)}) %collective-permute-start.6) | collective-permute-done | bytes 294944 | tf_op jit(solution)/shard_map/ppermute | solution.py:168
  322.9 6.8 %collective-permute-done.5 = bf16[2,96,768]{2,1,0:T(8,128)(2,1)S(1)} collective-permute-done((bf16[2,96,768]{2,1,0:T(8,128)(2,1)S(1)}, bf16[2,96,768]{2,1,0:T(8,128)(2,1)S(1)}, u32[]{:S(2)}, u32[]{:S(2)}) %collective-permute-start.5) | collective-permute-done | bytes 294944 | tf_op jit(solution)/shard_map/ppermute | solution.py:168
  330.4 0.7 gather_fusion
  331.5 0.8 copy.32
  332.3 1.2 copy.36
  333.5 0.8 copy.31
  334.3 1.2 copy.35
  (209 shorter events, 5.7 us)
Async XLA Ops:
  7.2 96.4 %all-gather.3.cloned.1.call-start = ((), (), s32[]{:S(2)}) async-start(), calls=%async_computation.7 | async-start | bytes 7077888 | tf_op jit(solution)/shard_map/all_gather | solution.py:99
  8.3 9.7 %collective-permute-start = (bf16[1,3,32,1536]{3,2,1,0:T(8,128)(2,1)S(1)}, bf16[1,3,32,1536]{3,2,1,0:T(8,128)(2,1)S(1)}, u32[]{:S(2)}, u32[]{:S(2)}) collective-permute-start(bf16[1,3,32,1536]{3,2,1,0:T(8,128)(2,1)S(1)} %get-tuple-element.135), channel_id=1, source_target_pairs={{0,1},{1,2},{2,3},{4,5},{5,6},{6,7},{8,9},{9,10},{10,11},{12,13},{... | collective-permute-start | bytes 884744 | tf_op jit(solution)/shard_map/ppermute | solution.py:35
  10.7 7.3 %collective-permute-start.1 = (bf16[1,3,32,1536]{3,2,1,0:T(8,128)(2,1)S(1)}, bf16[1,3,32,1536]{3,2,1,0:T(8,128)(2,1)S(1)}, u32[]{:S(2)}, u32[]{:S(2)}) collective-permute-start(bf16[1,3,32,1536]{3,2,1,0:T(8,128)(2,1)S(1)} %get-tuple-element.136), channel_id=1, source_target_pairs={{1,0},{2,1},{3,2},{5,4},{6,5},{7,6},{9,8},{10,9},{11,10},{13,12},{... | collective-permute-start | bytes 884744 | tf_op jit(solution)/shard_map/ppermute | solution.py:36
  13.4 15.3 %copy-start.8 = (f32[1536]{0:T(1024)}, f32[1536]{0:T(1024)S(1)}, u32[]{:S(2)}) copy-start(f32[1536]{0:T(1024)S(1)} %get-tuple-element.111) | copy-start | bytes 18436
  13.4 15.3 %copy-start.10 = (f32[1536]{0:T(1024)}, f32[1536]{0:T(1024)S(1)}, u32[]{:S(2)}) copy-start(f32[1536]{0:T(1024)S(1)} %get-tuple-element.112) | copy-start | bytes 18436
  13.4 15.3 %copy-start.11 = (f32[1536]{0:T(1024)}, f32[1536]{0:T(1024)S(1)}, u32[]{:S(2)}) copy-start(f32[1536]{0:T(1024)S(1)} %get-tuple-element.113) | copy-start | bytes 18436
  13.4 15.3 %copy-start.12 = (f32[1536]{0:T(1024)}, f32[1536]{0:T(1024)S(1)}, u32[]{:S(2)}) copy-start(f32[1536]{0:T(1024)S(1)} %get-tuple-element.114) | copy-start | bytes 18436
  13.5 15.3 %copy-start.13 = (f32[1536]{0:T(1024)}, f32[1536]{0:T(1024)S(1)}, u32[]{:S(2)}) copy-start(f32[1536]{0:T(1024)S(1)} %get-tuple-element.115) | copy-start | bytes 18436
  13.5 15.3 %copy-start.14 = (f32[1536]{0:T(1024)}, f32[1536]{0:T(1024)S(1)}, u32[]{:S(2)}) copy-start(f32[1536]{0:T(1024)S(1)} %get-tuple-element.116) | copy-start | bytes 18436
  13.5 15.3 %copy-start.15 = (f32[1536]{0:T(1024)}, f32[1536]{0:T(1024)S(1)}, u32[]{:S(2)}) copy-start(f32[1536]{0:T(1024)S(1)} %get-tuple-element.117) | copy-start | bytes 18436
  13.5 15.3 %copy-start.16 = (f32[1536]{0:T(1024)}, f32[1536]{0:T(1024)S(1)}, u32[]{:S(2)}) copy-start(f32[1536]{0:T(1024)S(1)} %get-tuple-element.118) | copy-start | bytes 18436
  13.5 15.3 %copy-start.17 = (f32[1536]{0:T(1024)}, f32[1536]{0:T(1024)S(1)}, u32[]{:S(2)}) copy-start(f32[1536]{0:T(1024)S(1)} %get-tuple-element.119) | copy-start | bytes 18436
  13.5 15.3 %copy-start.18 = (f32[1536]{0:T(1024)}, f32[1536]{0:T(1024)S(1)}, u32[]{:S(2)}) copy-start(f32[1536]{0:T(1024)S(1)} %get-tuple-element.120) | copy-start | bytes 18436
  15.4 13.4 %copy-start.19 = (f32[1536]{0:T(1024)}, f32[1536]{0:T(1024)S(1)}, u32[]{:S(2)}) copy-start(f32[1536]{0:T(1024)S(1)} %get-tuple-element.72) | copy-start | bytes 18436
  15.4 13.4 %copy-start.20 = (f32[1536]{0:T(1024)}, f32[1536]{0:T(1024)S(1)}, u32[]{:S(2)}) copy-start(f32[1536]{0:T(1024)S(1)} %get-tuple-element.73) | copy-start | bytes 18436
  15.4 13.4 %copy-start.21 = (f32[1536]{0:T(1024)}, f32[1536]{0:T(1024)S(1)}, u32[]{:S(2)}) copy-start(f32[1536]{0:T(1024)S(1)} %get-tuple-element.74) | copy-start | bytes 18436
  15.4 13.4 %copy-start.22 = (f32[1536]{0:T(1024)}, f32[1536]{0:T(1024)S(1)}, u32[]{:S(2)}) copy-start(f32[1536]{0:T(1024)S(1)} %get-tuple-element.75) | copy-start | bytes 18436
  15.4 13.4 %copy-start.23 = (f32[1536]{0:T(1024)}, f32[1536]{0:T(1024)S(1)}, u32[]{:S(2)}) copy-start(f32[1536]{0:T(1024)S(1)} %get-tuple-element.76) | copy-start | bytes 18436
  15.4 13.4 %copy-start.24 = (f32[1536]{0:T(1024)}, f32[1536]{0:T(1024)S(1)}, u32[]{:S(2)}) copy-start(f32[1536]{0:T(1024)S(1)} %get-tuple-element.77) | copy-start | bytes 18436
  15.4 13.4 %copy-start.25 = (f32[1536]{0:T(1024)}, f32[1536]{0:T(1024)S(1)}, u32[]{:S(2)}) copy-start(f32[1536]{0:T(1024)S(1)} %get-tuple-element.78) | copy-start | bytes 18436
  15.4 13.4 %copy-start.26 = (f32[1536]{0:T(1024)}, f32[1536]{0:T(1024)S(1)}, u32[]{:S(2)}) copy-start(f32[1536]{0:T(1024)S(1)} %get-tuple-element.79) | copy-start | bytes 18436
  15.4 13.4 %copy-start.27 = (f32[1536]{0:T(1024)}, f32[1536]{0:T(1024)S(1)}, u32[]{:S(2)}) copy-start(f32[1536]{0:T(1024)S(1)} %get-tuple-element.80) | copy-start | bytes 18436
  15.5 13.4 %copy-start.28 = (f32[1536]{0:T(1024)}, f32[1536]{0:T(1024)S(1)}, u32[]{:S(2)}) copy-start(f32[1536]{0:T(1024)S(1)} %get-tuple-element.81) | copy-start | bytes 18436
  15.5 13.4 %copy-start.29 = (f32[1536]{0:T(1024)}, f32[1536]{0:T(1024)S(1)}, u32[]{:S(2)}) copy-start(f32[1536]{0:T(1024)S(1)} %get-tuple-element.82) | copy-start | bytes 18436
  15.5 13.4 %copy-start.30 = (f32[1536]{0:T(1024)}, f32[1536]{0:T(1024)S(1)}, u32[]{:S(2)}) copy-start(f32[1536]{0:T(1024)S(1)} %get-tuple-element.83) | copy-start | bytes 18436
  15.5 13.4 %copy-start.31 = (f32[1536]{0:T(1024)}, f32[1536]{0:T(1024)S(1)}, u32[]{:S(2)}) copy-start(f32[1536]{0:T(1024)S(1)} %get-tuple-element.84) | copy-start | bytes 18436
  15.5 13.4 %copy-start.32 = (f32[1536]{0:T(1024)}, f32[1536]{0:T(1024)S(1)}, u32[]{:S(2)}) copy-start(f32[1536]{0:T(1024)S(1)} %get-tuple-element.85) | copy-start | bytes 18436
  15.5 13.4 %copy-start.33 = (f32[1536]{0:T(1024)}, f32[1536]{0:T(1024)S(1)}, u32[]{:S(2)}) copy-start(f32[1536]{0:T(1024)S(1)} %get-tuple-element.86) | copy-start | bytes 18436
  15.5 13.4 %copy-start.34 = (f32[1536]{0:T(1024)}, f32[1536]{0:T(1024)S(1)}, u32[]{:S(2)}) copy-start(f32[1536]{0:T(1024)S(1)} %get-tuple-element.87) | copy-start | bytes 18436
  15.5 13.4 %copy-start.35 = (f32[1536]{0:T(1024)}, f32[1536]{0:T(1024)S(1)}, u32[]{:S(2)}) copy-start(f32[1536]{0:T(1024)S(1)} %get-tuple-element.88) | copy-start | bytes 18436
  15.5 13.4 %copy-start.36 = (f32[1536]{0:T(1024)}, f32[1536]{0:T(1024)S(1)}, u32[]{:S(2)}) copy-start(f32[1536]{0:T(1024)S(1)} %get-tuple-element.89) | copy-start | bytes 18436
  15.5 13.4 %copy-start.37 = (f32[1536]{0:T(1024)}, f32[1536]{0:T(1024)S(1)}, u32[]{:S(2)}) copy-start(f32[1536]{0:T(1024)S(1)} %get-tuple-element.90) | copy-start | bytes 18436
  18.0 11.0 %copy-start.38 = (f32[1536]{0:T(1024)}, f32[1536]{0:T(1024)S(1)}, u32[]{:S(2)}) copy-start(f32[1536]{0:T(1024)S(1)} %get-tuple-element.91) | copy-start | bytes 18436
  18.0 11.0 %copy-start.39 = (f32[1536]{0:T(1024)}, f32[1536]{0:T(1024)S(1)}, u32[]{:S(2)}) copy-start(f32[1536]{0:T(1024)S(1)} %get-tuple-element.92) | copy-start | bytes 18436
  18.0 11.0 %copy-start.40 = (f32[1536]{0:T(1024)}, f32[1536]{0:T(1024)S(1)}, u32[]{:S(2)}) copy-start(f32[1536]{0:T(1024)S(1)} %get-tuple-element.93) | copy-start | bytes 18436
  18.0 11.0 %copy-start.41 = (f32[1536]{0:T(1024)}, f32[1536]{0:T(1024)S(1)}, u32[]{:S(2)}) copy-start(f32[1536]{0:T(1024)S(1)} %get-tuple-element.94) | copy-start | bytes 18436
  18.0 11.0 %copy-start.42 = (f32[1536]{0:T(1024)}, f32[1536]{0:T(1024)S(1)}, u32[]{:S(2)}) copy-start(f32[1536]{0:T(1024)S(1)} %get-tuple-element.95) | copy-start | bytes 18436
  18.0 11.0 %copy-start.43 = (f32[1536]{0:T(1024)}, f32[1536]{0:T(1024)S(1)}, u32[]{:S(2)}) copy-start(f32[1536]{0:T(1024)S(1)} %get-tuple-element.96) | copy-start | bytes 18436
  18.0 11.0 %copy-start.44 = (f32[1536]{0:T(1024)}, f32[1536]{0:T(1024)S(1)}, u32[]{:S(2)}) copy-start(f32[1536]{0:T(1024)S(1)} %get-tuple-element.97) | copy-start | bytes 18436
  18.0 11.0 %copy-start.45 = (f32[1536]{0:T(1024)}, f32[1536]{0:T(1024)S(1)}, u32[]{:S(2)}) copy-start(f32[1536]{0:T(1024)S(1)} %get-tuple-element.98) | copy-start | bytes 18436
  18.0 11.0 %copy-start.46 = (f32[1536]{0:T(1024)}, f32[1536]{0:T(1024)S(1)}, u32[]{:S(2)}) copy-start(f32[1536]{0:T(1024)S(1)} %get-tuple-element.99) | copy-start | bytes 18436
  18.0 11.0 %copy-start.47 = (f32[1536]{0:T(1024)}, f32[1536]{0:T(1024)S(1)}, u32[]{:S(2)}) copy-start(f32[1536]{0:T(1024)S(1)} %get-tuple-element.100) | copy-start | bytes 18436
  19.2 10.3 %copy-start.2 = (bf16[1,4,32,1536]{3,2,1,0:T(8,128)(2,1)S(1)}, bf16[1,4,32,1536]{3,2,1,0:T(8,128)(2,1)}, u32[]{:S(2)}) copy-start(bf16[1,4,32,1536]{3,2,1,0:T(8,128)(2,1)} %param.13) | copy-start | bytes 1179652
  19.2 10.3 %copy-start.7 = (f32[1536]{0:T(1024)S(1)}, f32[1536]{0:T(1024)}, u32[]{:S(2)}) copy-start(f32[1536]{0:T(1024)} %param.9) | copy-start | bytes 18436
  19.2 10.3 %copy-start.48 = (f32[1536]{0:T(1024)S(1)}, f32[1536]{0:T(1024)}, u32[]{:S(2)}) copy-start(f32[1536]{0:T(1024)} %param.12) | copy-start | bytes 18436
  31.9 17.6 %all-to-all-start.1 = ((bf16[4,768,96]{1,2,0:T(8,128)(2,1)}), bf16[4,768,96]{1,2,0:T(8,128)(2,1)S(1)}, u32[]{:S(2)}, u32[]{:S(2)}) async-start(bf16[4,768,96]{1,2,0:T(8,128)(2,1)} %bitcast.106), calls=%async_computation.1 | async-start | bytes 1179648 | tf_op jit(solution)/shard_map/all_to_all | solution.py:78
  52.4 51.2 %all-to-all-start = ((bf16[16,96,768]{2,1,0:T(8,128)(2,1)}), bf16[16,96,768]{2,1,0:T(8,128)(2,1)}, u32[]{:S(2)}, u32[]{:S(2)}) async-start(bf16[16,96,768]{2,1,0:T(8,128)(2,1)} %bitcast.98), calls=%async_computation | async-start | bytes 4718592 | tf_op jit(solution)/shard_map/all_to_all | solution.py:76
  57.7 96.6 %all-gather.5.cloned.1.call-start = ((), (), s32[]{:S(2)}) async-start(), calls=%async_computation.8 | async-start | bytes 2949120 | tf_op jit(solution)/shard_map/all_gather | solution.py:79
  58.5 174.5 %reduce-scatter.3.cloned.1.call-start = ((), (), s32[]{:S(2)}) async-start(), calls=%async_computation.9 | async-start | bytes 7077888 | tf_op jit(solution)/shard_map/reduce_scatter | solution.py:117
  161.0 5.2 %copy-start.62 = (bf16[1024,768]{1,0:T(8,128)(2,1)}, bf16[1024,768]{1,0:T(8,128)(2,1)S(1)}, u32[]{:S(2)}) copy-start(bf16[1024,768]{1,0:T(8,128)(2,1)S(1)} %fusion.7) | copy-start | bytes 4718596
  172.3 117.8 %reduce-scatter.5.cloned.1.call-start = ((), (), s32[]{:S(2)}) async-start(), calls=%async_computation.10 | async-start | bytes 2949120 | tf_op jit(solution)/shard_map/reduce_scatter | solution.py:129
  186.2 65.6 %all-to-all-start.2 = ((bf16[4,384,768]{2,1,0:T(8,128)(2,1)}), bf16[4,384,768]{2,1,0:T(8,128)(2,1)}, u32[]{:S(2)}, u32[]{:S(2)}) async-start(bf16[4,384,768]{2,1,0:T(8,128)(2,1)} %bitcast.104), calls=%async_computation.4 | async-start | bytes 4718592 | tf_op jit(solution)/shard_map/all_to_all | solution.py:128
  233.0 9.7 %copy-start = (bf16[2,128,1536]{2,1,0:T(8,128)(2,1)S(1)}, bf16[2,128,1536]{2,1,0:T(8,128)(2,1)}, u32[]{:S(2)}) copy-start(bf16[2,128,1536]{2,1,0:T(8,128)(2,1)} %reduce-scatter.3.cloned.1.call-done) | copy-start | bytes 2359300
  251.8 41.4 %all-to-all-start.3 = ((f32[32,2,1536]{2,1,0:T(2,128)}), f32[32,2,1536]{2,1,0:T(2,128)}, u32[]{:S(2)}, u32[]{:S(2)}) async-start(f32[32,2,1536]{2,1,0:T(2,128)} %reshape.621), calls=%async_computation.5 | async-start | bytes 786432 | tf_op jit(solution)/shard_map/all_to_all | solution.py:59
  256.6 34.7 %collective-permute-start.2 = (bf16[1,3,32,1536]{3,2,1,0:T(8,128)(2,1)S(1)}, bf16[1,3,32,1536]{3,2,1,0:T(8,128)(2,1)S(1)}, u32[]{:S(2)}, u32[]{:S(2)}) collective-permute-start(bf16[1,3,32,1536]{3,2,1,0:T(8,128)(2,1)S(1)} %get-tuple-element.133), channel_id=1, source_target_pairs={{0,1},{1,2},{2,3},{4,5},{5,6},{6,7},{8,9},{9,10},{10,11},{12,13},{... | collective-permute-start | bytes 884744 | tf_op jit(solution)/shard_map/ppermute | solution.py:35
  258.7 33.3 %collective-permute-start.3 = (bf16[1,3,32,1536]{3,2,1,0:T(8,128)(2,1)S(1)}, bf16[1,3,32,1536]{3,2,1,0:T(8,128)(2,1)}, u32[]{:S(2)}, u32[]{:S(2)}) collective-permute-start(bf16[1,3,32,1536]{3,2,1,0:T(8,128)(2,1)S(1)} %get-tuple-element.134), channel_id=1, source_target_pairs={{1,0},{2,1},{3,2},{5,4},{6,5},{7,6},{9,8},{10,9},{11,10},{13,12},{... | collective-permute-start | bytes 884744 | tf_op jit(solution)/shard_map/ppermute | solution.py:36
  291.3 8.7 %copy-start.9 = (f32[1536]{0:T(1024)S(1)}, f32[1536]{0:T(1024)}, u32[]{:S(2)}) copy-start(f32[1536]{0:T(1024)} %copy-done.8) | copy-start | bytes 18436
  295.2 18.0 %all-to-all-start.4 = ((f32[32,2,1536]{2,1,0:T(2,128)}), f32[32,2,1536]{2,1,0:T(2,128)S(1)}, u32[]{:S(2)}, u32[]{:S(2)}) async-start(f32[32,2,1536]{2,1,0:T(2,128)} %broadcast_in_dim.11), calls=%async_computation.6 | async-start | bytes 786432 | tf_op jit(solution)/shard_map/all_to_all | solution.py:61
  308.4 7.7 %copy-start.1 = (bf16[1,4,32,1536]{3,2,1,0:T(8,128)(2,1)S(1)}, bf16[1,4,32,1536]{3,2,1,0:T(8,128)(2,1)}, u32[]{:S(2)}) copy-start(bf16[1,4,32,1536]{3,2,1,0:T(8,128)(2,1)} %param.7) | copy-start | bytes 1179652
  308.4 7.7 %copy-start.3 = (f32[1,128,1536]{2,1,0:T(8,128)S(1)}, f32[1,128,1536]{2,1,0:T(8,128)}, u32[]{:S(2)}) copy-start(f32[1,128,1536]{2,1,0:T(8,128)} %get-tuple-element.132) | copy-start | bytes 2359300
  308.4 7.7 %copy-start.49 = (f32[1536]{0:T(1024)S(1)}, f32[1536]{0:T(1024)}, u32[]{:S(2)}) copy-start(f32[1536]{0:T(1024)} %param.12) | copy-start | bytes 18436
  315.0 8.0 %collective-permute-start.6 = (bf16[2,96,768]{2,1,0:T(8,128)(2,1)S(1)}, bf16[2,96,768]{2,1,0:T(8,128)(2,1)S(1)}, u32[]{:S(2)}, u32[]{:S(2)}) collective-permute-start(bf16[2,96,768]{2,1,0:T(8,128)(2,1)S(1)} %get-tuple-element.127), channel_id=1, source_target_pairs={{0,3},{1,0},{2,1},{3,2},{4,7},{5,4},{6,5},{7,6},{8,11},{9,8},{10,9... | collective-permute-start | bytes 884744 | tf_op jit(solution)/shard_map/ppermute | solution.py:168
  315.6 14.2 %collective-permute-start.5 = (bf16[2,96,768]{2,1,0:T(8,128)(2,1)S(1)}, bf16[2,96,768]{2,1,0:T(8,128)(2,1)S(1)}, u32[]{:S(2)}, u32[]{:S(2)}) collective-permute-start(bf16[2,96,768]{2,1,0:T(8,128)(2,1)S(1)} %get-tuple-element.128), channel_id=1, source_target_pairs={{0,2},{1,3},{2,0},{3,1},{4,6},{5,7},{6,4},{7,5},{8,10},{9,11},{10,... | collective-permute-start | bytes 884744 | tf_op jit(solution)/shard_map/ppermute | solution.py:168
  316.1 14.2 %collective-permute-start.4 = (bf16[2,96,768]{2,1,0:T(8,128)(2,1)S(1)}, bf16[2,96,768]{2,1,0:T(8,128)(2,1)S(1)}, u32[]{:S(2)}, u32[]{:S(2)}) collective-permute-start(bf16[2,96,768]{2,1,0:T(8,128)(2,1)S(1)} %get-tuple-element.129), channel_id=1, source_target_pairs={{0,1},{1,2},{2,3},{3,0},{4,5},{5,6},{6,7},{7,4},{8,9},{9,10},{10,1... | collective-permute-start | bytes 884744 | tf_op jit(solution)/shard_map/ppermute | solution.py:168
  (15 other events, 36.5 us)
Sparse Core Ops, SparseCore 0:
  30.9 67.5 all-gather.2
  100.7 53.6 all-gather.4
  172.4 60.5 reduce-scatter.2
  235.3 54.7 reduce-scatter.4
